TPU v7x, 256 devices: a whole 4x4x8 slice. The times are simulated.
256 devices in a mesh: wide: 32 (over z, x), narrow: 8 (over y, core).
Axes of the slice: x: 4, y: 4, z: 8, core: 2. Of those that a mesh axis runs over, the one named last changes fastest.
Arguments:
- hidden_in: bfloat16 [64, 8192], P(None, 'wide'), may hold values from -6 to 6
- attn_gain: bfloat16 [8192], P('wide'), may hold values from 0.099609375 to 1.8984375
- qkv_weight: bfloat16 [8192, 8, 10, 128], P('wide', 'narrow'), may hold values from -2 to 2
- qkv_bias: bfloat16 [8, 10, 128], P('narrow'), may hold values from -3 to 3
- cache_keys: bfloat16 [64, 8, 4096, 128], P('wide', 'narrow'), may hold values from -256 to 256
- cache_values: bfloat16 [64, 8, 4096, 128], P('wide', 'narrow'), may hold values from -10 to 10
- positions: int32 [64, 3, 4096], P('wide'), may hold values from 0 to 4095
- lengths: int32 [64], P('wide'), may hold values from 512 to 4095, as said below
- out_weight: bfloat16 [8192, 8192], P('narrow', 'wide'), may hold values from -0.0625 to 0.0625
- mlp_gain: bfloat16 [8192], P('wide'), may hold values from 0.099609375 to 1.8984375
- gate_up_weight: bfloat16 [8192, 2, 29568], P('wide', None, 'narrow'), may hold values from -0.0625 to 0.0625
- down_weight: bfloat16 [29568, 8192], P('narrow', 'wide'), may hold values from -0.03125 to 0.03125
Outputs:
- layer_out: bfloat16 [64, 8192], P(None, 'wide')
Inputs may be any that keep to these rules, and one draw needn't show every extreme that they name: Slots 0 to lengths[b] - 1 of request b are filled, the new token takes slot lengths[b], and some request has 4095.
All inputs are finite; a program needn't handle non-finite values.
Results may differ from a plain program's by a relative error of at most 0.01115.
The roundings to bfloat16 on the way count: a program that leaves them out, or rounds other values in their place, can miss the bound.
Values may be sent and summed in bfloat16 or wider, within the bound.
No kernel may reach another device: no remote copies, remote signals or barrier semaphores. Data moves between devices by JAX's collectives and lax.ppermute only.
A program may use at most 64 MiB of HBM per device.

v0:
```python
import math
import jax
import jax.numpy as jnp
from jax import lax
from jax.sharding import PartitionSpec as P

D = 8192
DH = 128
CACHE = 4096
norm_eps = 1e-06
rope_base = 1000000.0


def mrope_tables(position):
    half_width = DH // 2
    pair_index = jnp.arange(half_width)
    inv_freq = jnp.exp(pair_index.astype(jnp.float32) * (-2.0 * math.log(rope_base) / DH))
    component = (pair_index >= DH // 8).astype(jnp.int32) + (
        pair_index >= DH // 8 + 3 * DH // 16
    ).astype(jnp.int32)
    pos_float = position.astype(jnp.float32)
    chosen = jnp.where(
        component == 0,
        pos_float[..., 0, :, None],
        jnp.where(component == 1, pos_float[..., 1, :, None], pos_float[..., 2, :, None]),
    )
    angles = chosen * inv_freq
    return (jnp.cos(angles), jnp.sin(angles))


def rotate(values, cosine, sine_table):
    half_width = values.shape[-1] // 2
    leading = values[..., :half_width]
    trailing = values[..., half_width:]
    return jnp.concatenate(
        [leading * cosine - trailing * sine_table, trailing * cosine + leading * sine_table],
        axis=-1,
    )


def local(
    hidden_in,
    attn_gain,
    qkv_weight,
    qkv_bias,
    cache_keys,
    cache_values,
    positions,
    lengths,
    out_weight,
    mlp_gain,
    gate_up_weight,
    down_weight,
):
    score_scale = 1.0 / math.sqrt(DH)
    owned = lengths.shape[0]
    local_rows = hidden_in.shape[1]
    kv_local = qkv_weight.shape[1]
    slot_count = qkv_weight.shape[2]
    group_size = slot_count - 2
    width = kv_local * slot_count * DH
    inputs = hidden_in.astype(jnp.float32)
    local_squares = jnp.sum(inputs * inputs, axis=1)
    scaled = (inputs * attn_gain.astype(jnp.float32)).astype(jnp.bfloat16)
    weight_flat = qkv_weight.reshape(local_rows, width)
    partial = jnp.dot(scaled, weight_flat, preferred_element_type=jnp.float32)
    summed = lax.psum_scatter(
        jnp.concatenate([partial, local_squares[:, None]], axis=1),
        "wide",
        scatter_dimension=0,
        tiled=True,
    )
    inv_rms = 1.0 / jnp.sqrt(summed[:, width] / D + norm_eps)
    projected = inv_rms[:, None] * summed[:, :width] + qkv_bias.reshape(width).astype(jnp.float32)
    projected = projected.reshape(owned, kv_local, slot_count, DH)
    cosine, sine_table = mrope_tables(positions)
    keys_rot = rotate(cache_keys.astype(jnp.float32), cosine[:, None], sine_table[:, None]).astype(
        jnp.bfloat16
    )
    new_position = jnp.take_along_axis(positions, lengths[:, None, None], axis=2)
    cos_new, sin_new = mrope_tables(new_position)
    query = rotate(projected[:, :, :group_size], cos_new[:, None], sin_new[:, None]).astype(
        jnp.bfloat16
    )
    key_new = rotate(projected[:, :, group_size], cos_new, sin_new).astype(jnp.bfloat16)
    value_new = projected[:, :, group_size + 1].astype(jnp.bfloat16)
    scores = (
        jnp.einsum("rgjd,rgsd->rgjs", query, keys_rot, preferred_element_type=jnp.float32)
        * score_scale
    )
    own_score = (
        jnp.sum(query.astype(jnp.float32) * key_new.astype(jnp.float32)[:, :, None, :], axis=3)
        * score_scale
    )
    valid_slot = jnp.arange(CACHE)[None, None, None, :] < lengths[:, None, None, None]
    row_max = jnp.maximum(jnp.max(jnp.where(valid_slot, scores, -jnp.inf), axis=3), own_score)
    probabilities = jnp.where(valid_slot, jnp.exp(scores - row_max[..., None]), 0.0)
    own_prob = jnp.exp(own_score - row_max)
    totals = jnp.sum(probabilities, axis=3) + own_prob
    probs_rounded = probabilities.astype(jnp.bfloat16)
    own_rounded = own_prob.astype(jnp.bfloat16).astype(jnp.float32)
    weighted = jnp.einsum(
        "rgjs,rgsd->rgjd", probs_rounded, cache_values, preferred_element_type=jnp.float32
    )
    weighted = weighted + own_rounded[..., None] * value_new.astype(jnp.float32)[:, :, None, :]
    attended = (
        (weighted / totals[..., None])
        .astype(jnp.bfloat16)
        .reshape(owned, kv_local * group_size * DH)
    )
    head_partial = jnp.dot(
        lax.all_gather(attended, "wide", axis=0, tiled=True),
        out_weight,
        preferred_element_type=jnp.float32,
    )
    attn_out = lax.psum(head_partial, "narrow")
    residual = (inputs + attn_out).astype(jnp.bfloat16)
    resid_float = residual.astype(jnp.float32)
    resid_squares = jnp.sum(resid_float * resid_float, axis=1)
    scaled2 = (resid_float * mlp_gain.astype(jnp.float32)).astype(jnp.bfloat16)
    hidden_local = gate_up_weight.shape[2]
    gate_up_flat = gate_up_weight.reshape(local_rows, 2 * hidden_local)
    partial2 = jnp.dot(scaled2, gate_up_flat, preferred_element_type=jnp.float32)
    summed2 = lax.psum(jnp.concatenate([partial2, resid_squares[:, None]], axis=1), "wide")
    inv_rms2 = 1.0 / jnp.sqrt(summed2[:, 2 * hidden_local] / D + norm_eps)
    gate_up = summed2[:, : 2 * hidden_local] * inv_rms2[:, None]
    hidden = (jax.nn.silu(gate_up[:, :hidden_local]) * gate_up[:, hidden_local:]).astype(
        jnp.bfloat16
    )
    down_partial = jnp.dot(hidden, down_weight, preferred_element_type=jnp.float32)
    mlp_out = lax.psum(down_partial, "narrow")
    return (resid_float + mlp_out).astype(jnp.bfloat16)


def solution(mesh):
    in_specs = (
        P(None, "wide"),
        P("wide"),
        P("wide", "narrow", None, None),
        P("narrow", None, None),
        P("wide", "narrow", None, None),
        P("wide", "narrow", None, None),
        P("wide", None, None),
        P("wide"),
        P("narrow", "wide"),
        P("wide"),
        P("wide", None, "narrow"),
        P("narrow", "wide"),
    )
    out_specs = P(None, "wide")
    return jax.shard_map(local, mesh=mesh, in_specs=in_specs, out_specs=out_specs, check_vma=False)
```

profile of v0, /device:TPU:2, one launch (start us, length us, event | category | flops | bytes accessed | tf_op | source)
XLA Modules:
  0.0 506.0 jit_solution(6786295929845901364)
XLA Ops:
  6.5 1.0 fusion.28
  7.7 1.3 copy.24
  9.0 0.7 convert_element_type.170
  9.7 1.1 fusion.35
  10.8 0.8 pad_maximum_fusion.1
  11.7 2.7 copy.27
  14.5 3.8 bitcast_convert_fusion
  18.4 0.2 or_reduce_fusion
  18.6 1.4 gather_fusion
  20.1 0.2 slice_reduce_fusion.1
  20.3 0.1 fusion.61
  20.4 19.8 %fusion.7 = (bf16[2,4096,64]{2,1,0:T(8,128)(2,1)}, bf16[2,4096,64]{2,1,0:T(8,128)(2,1)}) fusion(f32[2,1,4096,128]{3,2,0,1:T(8,128)} %bitcast_convert_fusion, f32[64]{0:T(128)S(1)} %multiply_exponential_fusion, f32[2,4096]{1,0:T(2,128)S(1)} %get-tuple-element.17, f32[2,4096]{1,0:T(2,128)S(1)} %get-tuple-element.18, f32[2,4096]{1,0:T(2,128)S(1)} %get-tuple-element.16, ...), kind=kLoop, calls=%fused_computation.13 | loop fusion | flops 5767168 | bytes 6390144 | tf_op jit(solution)/shard_map/concatenate | solution.py:35
  40.4 0.6 dynamic-slice
  41.7 118.7 %all-reduce.12.cloned.1.call-done = f32[64,1281]{1,0:T(8,128)} async-done(((f32[64,1281]{1,0:T(8,128)}), f32[64,1281]{1,0:T(8,128)}) %all-reduce.12.cloned.1.call-update) | async-done | bytes 327952
  160.3 0.9 fusion.50
  161.2 0.9 fusion.42
  162.3 0.2 multiply_reduce_fusion
  162.5 3.6 select_reduce_fusion
  166.1 0.2 fusion.21
  166.3 0.4 fusion.15
  166.8 41.9 %all-gather = bf16[32,2,1024]{2,1,0:T(2,128)(2,1)S(1)} all-gather(bf16[1,2,1024]{2,1,0:T(2,128)(2,1)S(1)} %reshape.653), channel_id=1, replica_groups=mesh['wide'=32,'narrow'=8] {'wide'}, dimensions={0}, use_global_device_ids=true | all-gather | bytes 135168 | tf_op jit(solution)/shard_map/all_gather | solution.py:112
  208.7 0.8 fusion.62
  209.6 63.7 %all-reduce.6.cloned.1.call-done = f32[64,256]{1,0:T(8,128)} async-done(((f32[64,256]{1,0:T(8,128)}), f32[64,256]{1,0:T(8,128)}) %all-reduce.6.cloned.1.call-update) | async-done | bytes 65552 | tf_op jit(solution)/shard_map/psum | solution.py:116
  273.3 0.9 fusion.31
  274.3 3.4 fusion.33
  277.7 1.4 pad_maximum_fusion
  279.1 151.0 %all-reduce.8.cloned.1.call-done = f32[64,7393]{1,0:T(8,128)} async-done(((f32[64,7393]{1,0:T(8,128)}), f32[64,7393]{1,0:T(8,128)}) %all-reduce.8.cloned.1.call-update) | async-done | bytes 1892624 | tf_op jit(solution)/shard_map/psum | solution.py:124
  430.2 1.1 fusion.39
  431.2 1.7 slice_multiply_fusion
  433.0 1.2 fusion.19
  434.2 63.8 %all-reduce.10.cloned.1.call-done = f32[64,256]{1,0:T(8,128)} async-done(((f32[64,256]{1,0:T(8,128)}), f32[64,256]{1,0:T(8,128)}) %all-reduce.10.cloned.1.call-update) | async-done | bytes 65552 | tf_op jit(solution)/shard_map/psum | solution.py:131
  498.0 1.5 fusion.32
  (53 shorter events, 1.3 us)
Async XLA Ops:
  6.5 159.8 %copy-start = (bf16[2,1,4096,128]{3,2,1,0:T(8,128)(2,1)S(1)}, bf16[2,1,4096,128]{3,2,1,0:T(8,128)(2,1)}, u32[]{:S(2)}) copy-start(bf16[2,1,4096,128]{3,2,1,0:T(8,128)(2,1)} %param.17) | copy-start | bytes 6291460
  6.5 5.1 %copy-start.2 = (s32[2,3,4096]{2,0,1:T(2,128)S(1)}, s32[2,3,4096]{2,0,1:T(2,128)}, u32[]{:S(2)}) copy-start(s32[2,3,4096]{2,0,1:T(2,128)} %param.18) | copy-start | bytes 294916
  6.5 153.8 %all-reduce.12.cloned.1.call-start = ((), (), s32[]{:S(2)}) async-start(), calls=%async_computation.3 | async-start | bytes 720896
  11.6 261.7 %all-reduce.6.cloned.1.call-start = ((), (), s32[]{:S(2)}) async-start(), calls=%async_computation | async-start | bytes 131072 | tf_op jit(solution)/shard_map/psum | solution.py:116
  11.7 2.7 copy-start.5
  20.4 20.0 %copy-start.8 = (u32[256]{0:T(256)S(1)}, u32[256]{0:T(256)}, u32[]{:S(2)}) copy-start(u32[256]{0:T(256)} %constant.64) | copy-start | bytes 3076
  20.4 21.2 %copy-start.4 = (bf16[1,10,128]{2,1,0:T(8,128)(2,1)S(1)}, bf16[1,10,128]{2,1,0:T(8,128)(2,1)}, u32[]{:S(2)}) copy-start(bf16[1,10,128]{2,1,0:T(8,128)(2,1)} %param.15) | copy-start | bytes 7684
  166.0 42.6 %copy-start.1 = (bf16[1024,256]{1,0:T(8,128)(2,1)S(1)}, bf16[1024,256]{1,0:T(8,128)(2,1)}, u32[]{:S(2)}) copy-start(bf16[1024,256]{1,0:T(8,128)(2,1)} %param.20) | copy-start | bytes 1572868
  166.0 43.5 %copy-start.7 = (bf16[256]{0:T(256)(128)(2,1)S(1)}, bf16[256]{0:T(256)(128)(2,1)}, u32[]{:S(2)}) copy-start(bf16[256]{0:T(256)(128)(2,1)} %param.21) | copy-start | bytes 1540
  166.0 107.2 %copy-start.3 = (bf16[64,256]{1,0:T(8,128)(2,1)S(1)}, bf16[64,256]{1,0:T(8,128)(2,1)}, u32[]{:S(2)}) copy-start(bf16[64,256]{1,0:T(8,128)(2,1)} %param.12) | copy-start | bytes 98308
  209.5 220.6 %all-reduce.8.cloned.1.call-start = ((), (), s32[]{:S(2)}) async-start(), calls=%async_computation.1 | async-start | bytes 3801088 | tf_op jit(solution)/shard_map/psum | solution.py:124
  279.1 218.9 %all-reduce.10.cloned.1.call-start = ((), (), s32[]{:S(2)}) async-start(), calls=%async_computation.2 | async-start | bytes 131072 | tf_op jit(solution)/shard_map/psum | solution.py:131
  430.2 2.8 copy-start.6
Sparse Core Ops, SparseCore 0:
  11.7 148.5 all-reduce.11
  209.6 63.5 all-reduce.5
  279.2 150.9 all-reduce.7
  434.3 63.6 all-reduce.9
where the time goes:
time: 507 us; the launch traced here: 506 us
  waiting for transfers between devices  397 us (78%)
  blocking collectives  41.9 us (8%)
  other arithmetic  35.6 us (7%)
  between operations  14 us (3%)
  matrix products  10.4 us (2%)
  local copies, waits for them, and re-layouts  6.65 us (1%)
    psum x1, waiting for transfers between devices, local(): lax.psum(jnp.concatenate([partial2, resid_squares[:, None]], axis=1), 'wi...  151 us
    unnamed x5, waiting for transfers between devices  119 us
    psum x1, waiting for transfers between devices, local(): mlp_out = lax.psum(down_partial, 'narrow')  63.8 us
    psum x1, waiting for transfers between devices, local(): attn_out = lax.psum(head_partial, 'narrow')  63.7 us
    all_gather x1, blocking collectives, local(): lax.all_gather(attended, 'wide', axis=0, tiled=True)  41.9 us
    concatenate x2, other arithmetic, rotate(): jnp.concatenate([leading * cosine - trailing * sine_table, trailing * cos...  19.8 us
  transfers between devices with their start and end apart: 4, of which 4 were waited for; matrix products, arithmetic and copies ran while one was open for 6% of the time, Pallas kernels for 0%

commit v1 on v0

--- a/solution.py
+++ b/solution.py
@@ -113,7 +113,7 @@
         out_weight,
         preferred_element_type=jnp.float32,
     )
-    attn_out = lax.psum(head_partial, "narrow")
+    attn_out = jnp.sum(lax.all_gather(head_partial, "narrow"), axis=0)
     residual = (inputs + attn_out).astype(jnp.bfloat16)
     resid_float = residual.astype(jnp.float32)
     resid_squares = jnp.sum(resid_float * resid_float, axis=1)

time: 507 us -> 454 us (0.90)
  waiting for transfers between devices: 397 us -> 333 us
  blocking collectives: 41.9 us -> 55.3 us
    psum x1 -> x0, waiting for transfers between devices: 63.7 us -> none  [local(): attn_out = lax.psum(head_partial, 'narrow')]
    all_gather x0 -> x1, blocking collectives: none -> 13.4 us  [local(): attn_out = jnp.sum(lax.all_gather(head_partial, 'narrow'), axis=0)]
    unnamed x5 -> x4, waiting for transfers between devices: 119 us -> 119 us
  transfers between devices with their start and end apart: 4 -> 3, of which waited for: 4 -> 3; matrix products, arithmetic and copies ran while one was open for 6% -> 6% of each run, Pallas kernels for 0% -> 0%
where the time goes in v1:
time: 454 us; the launch traced here: 453 us
  waiting for transfers between devices  333 us (73%)
  blocking collectives  55.3 us (12%)
  other arithmetic  34.8 us (8%)
  between operations  14 us (3%)
  matrix products  9.82 us (2%)
  local copies, waits for them, and re-layouts  6.65 us (1%)
    psum x1, waiting for transfers between devices, local(): lax.psum(jnp.concatenate([partial2, resid_squares[:, None]], axis=1), 'wi...  150 us
    unnamed x4, waiting for transfers between devices  119 us
    psum x1, waiting for transfers between devices, local(): mlp_out = lax.psum(down_partial, 'narrow')  63.8 us
    all_gather x1, blocking collectives, local(): lax.all_gather(attended, 'wide', axis=0, tiled=True)  41.9 us
    concatenate x2, other arithmetic, rotate(): jnp.concatenate([leading * cosine - trailing * sine_table, trailing * cos...  19.8 us
    all_gather x1, blocking collectives, local(): attn_out = jnp.sum(lax.all_gather(head_partial, 'narrow'), axis=0)  13.4 us
  transfers between devices with their start and end apart: 3, of which 3 were waited for; matrix products, arithmetic and copies ran while one was open for 6% of the time, Pallas kernels for 0%

profile of v1, /device:TPU:2, one launch (start us, length us, event | category | flops | bytes accessed | tf_op | source)
XLA Modules:
  0.0 453.3 jit_solution(2820658217397555160)
XLA Ops:
  6.5 1.0 fusion.28
  7.7 1.3 copy.24
  9.0 0.7 convert_element_type.170
  9.7 1.1 fusion.35
  10.8 0.8 pad_maximum_fusion.1
  11.7 2.7 copy.27
  14.5 3.8 bitcast_convert_fusion
  18.4 0.2 or_reduce_fusion
  18.6 1.4 gather_fusion
  20.1 0.2 slice_reduce_fusion.1
  20.3 0.1 fusion.61
  20.5 19.8 %fusion.7 = (bf16[2,4096,64]{2,1,0:T(8,128)(2,1)}, bf16[2,4096,64]{2,1,0:T(8,128)(2,1)}) fusion(f32[2,1,4096,128]{3,2,0,1:T(8,128)} %bitcast_convert_fusion, f32[64]{0:T(128)S(1)} %multiply_exponential_fusion, f32[2,4096]{1,0:T(2,128)S(1)} %get-tuple-element.17, f32[2,4096]{1,0:T(2,128)S(1)} %get-tuple-element.18, f32[2,4096]{1,0:T(2,128)S(1)} %get-tuple-element.16, ...), kind=kLoop, calls=%fused_computation.13 | loop fusion | flops 5767168 | bytes 6390144 | tf_op jit(solution)/shard_map/concatenate | solution.py:35
  40.4 0.6 dynamic-slice
  41.7 118.6 %all-reduce.9.cloned.1.call-done = f32[64,1281]{1,0:T(8,128)} async-done(((f32[64,1281]{1,0:T(8,128)}), f32[64,1281]{1,0:T(8,128)}) %all-reduce.9.cloned.1.call-update) | async-done | bytes 327952
  160.3 0.9 fusion.50
  161.2 0.9 fusion.42
  162.3 0.2 multiply_reduce_fusion
  162.5 3.6 select_reduce_fusion
  166.0 0.2 fusion.21
  166.3 0.4 fusion.15
  166.8 41.9 %all-gather.1 = bf16[32,2,1024]{2,1,0:T(2,128)(2,1)S(1)} all-gather(bf16[1,2,1024]{2,1,0:T(2,128)(2,1)S(1)} %reshape.654), channel_id=1, replica_groups=mesh['wide'=32,'narrow'=8] {'wide'}, dimensions={0}, use_global_device_ids=true | all-gather | bytes 135168 | tf_op jit(solution)/shard_map/all_gather | solution.py:112
  208.7 0.2 fusion.62
  208.9 13.4 %all-gather = f32[512,256]{1,0:T(8,128)S(1)} all-gather(f32[64,256]{1,0:T(8,128)S(1)} %fusion.62), channel_id=2, replica_groups=mesh['wide'=32,'narrow'=8] {'narrow'}, dimensions={0}, use_global_device_ids=true | all-gather | bytes 589824 | tf_op jit(solution)/shard_map/all_gather | solution.py:116
  222.4 0.1 fusion.31
  222.6 3.3 fusion.33
  225.9 1.4 pad_maximum_fusion
  227.4 150.1 %all-reduce.5.cloned.1.call-done = f32[64,7393]{1,0:T(8,128)} async-done(((f32[64,7393]{1,0:T(8,128)}), f32[64,7393]{1,0:T(8,128)}) %all-reduce.5.cloned.1.call-update) | async-done | bytes 1892624 | tf_op jit(solution)/shard_map/psum | solution.py:124
  377.5 1.1 fusion.39
  378.6 1.7 slice_multiply_fusion
  380.3 1.2 fusion.19
  381.5 63.8 %all-reduce.7.cloned.1.call-done = f32[64,256]{1,0:T(8,128)} async-done(((f32[64,256]{1,0:T(8,128)}), f32[64,256]{1,0:T(8,128)}) %all-reduce.7.cloned.1.call-update) | async-done | bytes 65552 | tf_op jit(solution)/shard_map/psum | solution.py:131
  445.3 1.5 fusion.32
  (52 shorter events, 1.2 us)
Async XLA Ops:
  6.5 159.7 %copy-start = (bf16[2,1,4096,128]{3,2,1,0:T(8,128)(2,1)S(1)}, bf16[2,1,4096,128]{3,2,1,0:T(8,128)(2,1)}, u32[]{:S(2)}) copy-start(bf16[2,1,4096,128]{3,2,1,0:T(8,128)(2,1)} %param.17) | copy-start | bytes 6291460
  6.5 5.1 %copy-start.2 = (s32[2,3,4096]{2,0,1:T(2,128)S(1)}, s32[2,3,4096]{2,0,1:T(2,128)}, u32[]{:S(2)}) copy-start(s32[2,3,4096]{2,0,1:T(2,128)} %param.18) | copy-start | bytes 294916
  6.5 153.8 %all-reduce.9.cloned.1.call-start = ((), (), s32[]{:S(2)}) async-start(), calls=%async_computation.2 | async-start | bytes 720896
  11.6 365.9 %all-reduce.5.cloned.1.call-start = ((), (), s32[]{:S(2)}) async-start(), calls=%async_computation | async-start | bytes 3801088 | tf_op jit(solution)/shard_map/psum | solution.py:124
  11.7 2.7 copy-start.5
  20.4 20.0 %copy-start.7 = (bf16[256]{0:T(256)(128)(2,1)S(1)}, bf16[256]{0:T(256)(128)(2,1)}, u32[]{:S(2)}) copy-start(bf16[256]{0:T(256)(128)(2,1)} %param.21) | copy-start | bytes 1540
  20.4 20.0 %copy-start.8 = (u32[256]{0:T(256)S(1)}, u32[256]{0:T(256)}, u32[]{:S(2)}) copy-start(u32[256]{0:T(256)} %constant.64) | copy-start | bytes 3076
  20.4 21.2 %copy-start.4 = (bf16[1,10,128]{2,1,0:T(8,128)(2,1)S(1)}, bf16[1,10,128]{2,1,0:T(8,128)(2,1)}, u32[]{:S(2)}) copy-start(bf16[1,10,128]{2,1,0:T(8,128)(2,1)} %param.15) | copy-start | bytes 7684
  166.0 42.6 %copy-start.1 = (bf16[1024,256]{1,0:T(8,128)(2,1)S(1)}, bf16[1024,256]{1,0:T(8,128)(2,1)}, u32[]{:S(2)}) copy-start(bf16[1024,256]{1,0:T(8,128)(2,1)} %param.20) | copy-start | bytes 1572868
  166.3 56.1 %copy-start.3 = (bf16[64,256]{1,0:T(8,128)(2,1)S(1)}, bf16[64,256]{1,0:T(8,128)(2,1)}, u32[]{:S(2)}) copy-start(bf16[64,256]{1,0:T(8,128)(2,1)} %param.12) | copy-start | bytes 98308
  227.3 218.0 %all-reduce.7.cloned.1.call-start = ((), (), s32[]{:S(2)}) async-start(), calls=%async_computation.1 | async-start | bytes 131072 | tf_op jit(solution)/shard_map/psum | solution.py:131
  377.5 2.8 copy-start.6
Sparse Core Ops, SparseCore 0:
  11.7 148.5 all-reduce.8
  227.5 149.9 all-reduce.4
  381.6 63.6 all-reduce.6
